TPU v7x, 256 devices: a whole 4x4x8 slice. The times are simulated.
256 devices in a mesh: docs: 32 (over y, x, z_hi), dims: 8 (over z_lo, core).
Axes of the slice: x: 4, y: 4, z: 8 (z_hi: 2, z_lo: 4; z = z_hi * 4 + z_lo), core: 2. Of those that a mesh axis runs over, the one named last changes fastest.
Arguments:
- queries: bfloat16 [16384, 3072], P('docs', 'dims'), may hold values from -6 to 6
- doc_vectors: bfloat16 [65536, 3072], P('docs', 'dims'), may hold values from -6 to 6
- surv_pairs: int32 [32, 144], P('docs'), may hold values from 0 to 2047
- surv_count: int32 [32], P('docs'), may hold values from 36 to 144, as said below
- short_pairs: int32 [32, 96], P('docs'), may hold values from 0 to 2047
- short_count: int32 [32], P('docs'), may hold values from 24 to 96, as said below
Outputs:
- prefix_scores: float32 [32, 144, 128, 128], P('docs', None, 'dims')
- full_scores: float32 [32, 96, 128, 128], P('docs', None, 'dims')
Inputs may be any that keep to these rules, and one draw needn't show every extreme that they name: `surv_count`: each shard's live survivor slots; some shard has all 144 slots live. `short_count`: each shard's live shortlist slots; some shard has all 96 slots live.
All inputs are finite; a program needn't handle non-finite values.
Results may differ from a plain program's by a relative error of at most 0.0003.
Values may be sent and summed in bfloat16 or wider, within the bound.
No kernel may reach another device: no remote copies, remote signals or barrier semaphores. Data moves between devices by JAX's collectives and lax.ppermute only.
A program may use at most 128 MiB of HBM per device.

v0:
```python
import jax
import jax.numpy as jnp
from jax import lax
from jax.sharding import Mesh
from jax.sharding import PartitionSpec as P

D = 3072
PREFIX = 768
QB = 128
DB = 128
DOCS_PARTS = (("y", 4), ("x", 4), ("zh", 2))
DIMS_PARTS = (("zl", 4), ("c", 2))
DOCS = tuple((name for name, _ in DOCS_PARTS))
DIMS = tuple((name for name, _ in DIMS_PARTS))


def shards(queries, doc_vectors, surv_pairs, surv_count, short_pairs, short_count):
    near = lax.all_gather(queries, "zh", axis=0, tiled=True)
    every_query = lax.all_gather(near, ("y", "x"), axis=0, tiled=True)
    slice_width = queries.shape[1]
    query_blocks = every_query.reshape(-1, QB, slice_width)
    doc_blocks = doc_vectors.reshape(-1, DB, slice_width)
    local_blocks = doc_blocks.shape[0]
    columns = lax.axis_index(DIMS) * slice_width + jnp.arange(slice_width)
    prefix_blocks = jnp.where(
        columns[None, None, :] < PREFIX, doc_blocks, jnp.zeros((), doc_blocks.dtype)
    )

    def pair_products(pair_ids, doc_side):
        picked_queries = jnp.take(query_blocks, pair_ids // local_blocks, axis=0)
        picked_docs = jnp.take(doc_side, pair_ids % local_blocks, axis=0)
        return jnp.einsum(
            "gqc,gdc->gqd", picked_queries, picked_docs, preferred_element_type=jnp.float32
        )

    full_terms = pair_products(short_pairs[0], doc_blocks)
    prefix_terms = pair_products(surv_pairs[0], prefix_blocks)
    prefix_sum, full_sum = (
        lax.psum_scatter(prefix_terms, DIMS, scatter_dimension=1, tiled=True),
        lax.psum_scatter(full_terms, DIMS, scatter_dimension=1, tiled=True),
    )

    def finish(summed, live_count, factor):
        slots = jnp.arange(summed.shape[0])
        return jnp.where(slots[:, None, None] < live_count, summed * factor, jnp.float32(0.0))

    prefix_out = finish(prefix_sum, surv_count[0], float(PREFIX) ** (-0.5))
    full_out = finish(full_sum, short_count[0], float(D) ** (-0.5))
    return (prefix_out[None], full_out[None])


def solution(mesh):
    sizes = [n for _, n in DOCS_PARTS + DIMS_PARTS]
    assert mesh.devices.size == jnp.prod(jnp.array(sizes))
    parts = Mesh(mesh.devices.reshape(sizes), DOCS + DIMS)
    placed = (P(DOCS, DIMS), P(DOCS, DIMS), P(DOCS, None), P(DOCS), P(DOCS, None), P(DOCS))
    return jax.shard_map(
        shards,
        mesh=parts,
        in_specs=placed,
        out_specs=(P(DOCS, None, DIMS, None), P(DOCS, None, DIMS, None)),
        check_vma=False,
    )
```

profile of v0, /device:TPU:2, one launch (start us, length us, event | category | flops | bytes accessed | tf_op | source)
XLA Modules:
  0.0 341.6 jit_solution(15398356191512357973)
XLA Ops:
  7.2 0.0 all-gather.2.cloned.1.call-start
  7.2 23.2 %all_gather.6 = bf16[1024,384]{1,0:T(8,128)(2,1)} all-gather(bf16[512,384]{1,0:T(8,128)(2,1)} %param.6), channel_id=1, replica_groups=mesh['y'=4,'x'=4,'zh'=2,'zl'=4,'c'=2] {'zh'}, dimensions={0}, use_global_device_ids=true | all-gather | bytes 1179648 | tf_op jit(solution)/shard_map/all_gather | solution.py:18
  30.4 0.0 all-gather.2.cloned.1.call-update
  30.5 0.0 reduce-scatter.5.cloned.1.call-start
  30.5 0.7 fusion.12
  31.2 0.0 copy-start.2
  31.2 9.3 %gather_fusion.3 = bf16[96,128,384]{2,1,0:T(8,128)(2,1)} fusion(bf16[16,128,384]{2,1,0:T(8,128)(2,1)} %bitcast.65, s32[1024]{0:T(1024)S(1)} %get-tuple-element.10), kind=kCustom, calls=%fused_computation.3 | custom fusion | bytes 18874752 | tf_op jit(solution)/shard_map/jit(_take)/gather | solution.py:31
  40.5 0.0 copy-done.2
  40.5 88.3 %all-gather.2.cloned.1.call-done = bf16[16384,384]{1,0:T(8,128)(2,1)} async-done(((bf16[1024,384]{1,0:T(8,128)(2,1)}), bf16[16384,384]{1,0:T(8,128)(2,1)}) %all-gather.2.cloned.1.call-update) | async-done | bytes 12582928 | tf_op jit(solution)/shard_map/all_gather | solution.py:19
  128.9 12.5 %gather_fusion.2 = bf16[96,128,384]{2,1,0:T(8,128)(2,1)} fusion(bf16[128,128,384]{2,1,0:T(8,128)(2,1)} %bitcast.67, s32[1024]{0:T(1024)S(1)} %get-tuple-element.11), kind=kCustom, calls=%fused_computation.2 | custom fusion | bytes 18874752 | tf_op jit(solution)/shard_map/jit(_take)/gather | solution.py:30
  141.3 0.0 copy-start.1
  141.3 0.0 copy-start
  141.4 10.4 %fusion.5 = f32[96,128,128]{2,1,0:T(8,128)} fusion(bf16[96,128,384]{2,1,0:T(8,128)(2,1)} %gather_fusion.3, bf16[96,128,384]{2,1,0:T(8,128)(2,1)} %gather_fusion.2, pred[96]{0:T(512)(128)(4,1)S(1)} %get-tuple-element.7, pred[96]{0:T(512)(128)(4,1)S(1)} %get-tuple-element.6), kind=kOutput, calls=%fused_computation.9 | convolution fusion | flops 1217396736 | bytes 25166016 | tf_op jit(solution)/shard_map/gqc,gdc->gqd/dot_general | solution.py:32
  151.8 0.0 reduce-scatter.5.cloned.1.call-update
  151.8 0.2 reduce-scatter.3.cloned.1.call-start
  152.1 0.0 copy-done.1
  152.1 0.0 copy-done
  152.1 0.2 broadcast_select_fusion
  152.3 9.5 %gather_fusion.1 = bf16[144,128,384]{2,1,0:T(8,128)(2,1)} fusion(bf16[16,128,384]{2,1,0:T(8,128)(2,1)S(1)} %broadcast_select_fusion, s32[1024]{0:T(1024)S(1)} %pad_clamp_fusion.2), kind=kCustom, calls=%fused_computation.1 | custom fusion | bytes 28312128 | tf_op jit(solution)/shard_map/jit(_take)/gather | solution.py:31
  161.8 14.7 %gather_fusion = bf16[144,128,384]{2,1,0:T(8,128)(2,1)} fusion(bf16[128,128,384]{2,1,0:T(8,128)(2,1)} %bitcast.68, s32[1024]{0:T(1024)S(1)} %pad_clamp_fusion.3), kind=kCustom, calls=%fused_computation | custom fusion | bytes 28312128 | tf_op jit(solution)/shard_map/jit(_take)/gather | solution.py:30
  176.5 14.9 %fusion = f32[144,128,128]{2,1,0:T(8,128)} fusion(bf16[144,128,384]{2,1,0:T(8,128)(2,1)} %gather_fusion.1, bf16[144,128,384]{2,1,0:T(8,128)(2,1)} %gather_fusion, pred[144]{0:T(512)(128)(4,1)S(1)} %get-tuple-element.5, pred[144]{0:T(512)(128)(4,1)S(1)} %get-tuple-element.4), kind=kOutput, calls=%fused_computation.4 | convolution fusion | flops 1826095104 | bytes 37749024 | tf_op jit(solution)/shard_map/gqc,gdc->gqd/dot_general | solution.py:32
  191.4 0.0 reduce-scatter.3.cloned.1.call-update
  192.7 34.0 %reduce-scatter.5.cloned.1.call-done = f32[96,16,128]{2,1,0:T(8,128)} async-done(((f32[96,128,128]{2,1,0:T(8,128)}), f32[96,16,128]{2,1,0:T(8,128)}) %reduce-scatter.5.cloned.1.call-update) | async-done | bytes 786448 | tf_op jit(solution)/shard_map/reduce_scatter | solution.py:40
  226.7 2.2 select_bitcast_fusion.1
  228.9 103.7 %reduce-scatter.3.cloned.1.call-done = f32[144,16,128]{2,1,0:T(8,128)} async-done(((f32[144,128,128]{2,1,0:T(8,128)}), f32[144,16,128]{2,1,0:T(8,128)}) %reduce-scatter.3.cloned.1.call-update) | async-done | bytes 1179664 | tf_op jit(solution)/shard_map/reduce_scatter | solution.py:39
  332.6 2.5 select_bitcast_fusion
  (10 shorter events, 0.1 us)
Async XLA Ops:
  7.2 121.7 %all-gather.2.cloned.1.call-start = ((), (), s32[]{:S(2)}) async-start(), calls=%async_computation.2 | async-start | bytes 13369344 | tf_op jit(solution)/shard_map/all_gather | solution.py:19
  30.5 196.3 %reduce-scatter.5.cloned.1.call-start = ((), (), s32[]{:S(2)}) async-start(), calls=%async_computation.4 | async-start | bytes 7077888 | tf_op jit(solution)/shard_map/reduce_scatter | solution.py:40
  31.2 9.3 %copy-start.2 = (s32[1,96]{1,0:T(1,128)S(1)}, s32[1,96]{1,0:T(1,128)}, u32[]{:S(2)}) copy-start(s32[1,96]{1,0:T(1,128)} %param.10) | copy-start | bytes 1156
  141.3 10.7 %copy-start.1 = (s32[1,144]{1,0:T(1,128)S(1)}, s32[1,144]{1,0:T(1,128)}, u32[]{:S(2)}) copy-start(s32[1,144]{1,0:T(1,128)} %param.8) | copy-start | bytes 1732
  141.3 10.8 %copy-start = (bf16[2048,384]{1,0:T(8,128)(2,1)S(1)}, bf16[2048,384]{1,0:T(8,128)(2,1)}, u32[]{:S(2)}) copy-start(bf16[2048,384]{1,0:T(8,128)(2,1)} %param.7) | copy-start | bytes 4718596
  151.8 180.8 %reduce-scatter.3.cloned.1.call-start = ((), (), s32[]{:S(2)}) async-start(), calls=%async_computation.3 | async-start | bytes 10616832 | tf_op jit(solution)/shard_map/reduce_scatter | solution.py:39
Sparse Core Ops, SparseCore 0:
  30.6 98.2 all-gather.1
  151.9 74.7 reduce-scatter.4
  229.3 103.2 reduce-scatter.2
where the time goes:
time: 342 us
  waiting for transfers between devices  226 us (66%)
  local copies, waits for them, and re-layouts  46 us (13%)
  matrix products  25.3 us (7%)
  blocking collectives  23.2 us (7%)
  between operations  15.1 us (4%)
  other arithmetic  5.6 us (2%)
    reduce_scatter x1, waiting for transfers between devices, shards(): lax.psum_scatter(prefix_terms, DIMS, scatter_dimension=1, tiled=True)  104 us
    all_gather x1, waiting for transfers between devices, shards(): every_query = lax.all_gather(near, ('y', 'x'), axis=0, tiled=True)  88.3 us
    reduce_scatter x1, waiting for transfers between devices, shards(): lax.psum_scatter(full_terms, DIMS, scatter_dimension=1, tiled=True)  34 us
    gather x2, local copies, waits for them, and re-layouts, pair_products(): picked_queries = jnp.take(query_blocks, pair_ids // local_blocks, axis=0)  27.2 us
    dot_general x2, matrix products, pair_products(): jnp.einsum('gqc,gdc->gqd', picked_queries, picked_docs, preferred_element...  25.3 us
    all_gather x1, blocking collectives, shards(): near = lax.all_gather(queries, 'zh', axis=0, tiled=True)  23.2 us
    gather x2, local copies, waits for them, and re-layouts, pair_products(): picked_docs = jnp.take(doc_side, pair_ids % local_blocks, axis=0)  18.8 us
  transfers between devices with their start and end apart: 3, of which 3 were waited for; matrix products, arithmetic and copies ran while one was open for 15% of the time, Pallas kernels for 0%

commit v1 on v0

--- a/solution.py
+++ b/solution.py
@@ -15,7 +15,13 @@
 
 
 def shards(queries, doc_vectors, surv_pairs, surv_count, short_pairs, short_count):
-    near = lax.all_gather(queries, "zh", axis=0, tiled=True)
+    wide_out = jax.lax.all_to_all(
+        jnp.stack([queries for _ in range(jax.lax.psum(1, axis_name="zh"))], axis=0),
+        axis_name="zh",
+        split_axis=0,
+        concat_axis=0,
+    )
+    near = jnp.concatenate(wide_out, axis=0)
     every_query = lax.all_gather(near, ("y", "x"), axis=0, tiled=True)
     slice_width = queries.shape[1]
     query_blocks = every_query.reshape(-1, QB, slice_width)

time: 342 us -> 345 us (level)
  blocking collectives: 23.2 us -> 30.6 us
  waiting for transfers between devices: 226 us -> 222 us
    all_to_all x0 -> x1, blocking collectives: none -> 30.6 us  [shards(): jax.lax.all_to_all(jnp.stack([queries for _ in range(jax.lax.psum(1, axis...]
    all_gather x1 -> x0, blocking collectives: 23.2 us -> none  [shards(): near = lax.all_gather(queries, 'zh', axis=0, tiled=True)]
    all_gather x1, waiting for transfers between devices: 88.3 us -> 84.3 us  [shards(): every_query = lax.all_gather(near, ('y', 'x'), axis=0, tiled=True)]
where the time goes in v1:
time: 345 us
  waiting for transfers between devices  222 us (64%)
  local copies, waits for them, and re-layouts  44.6 us (13%)
  blocking collectives  30.6 us (9%)
  matrix products  25.2 us (7%)
  between operations  15.1 us (4%)
  other arithmetic  6.91 us (2%)
    reduce_scatter x1, waiting for transfers between devices, shards(): lax.psum_scatter(prefix_terms, DIMS, scatter_dimension=1, tiled=True)  104 us
    all_gather x1, waiting for transfers between devices, shards(): every_query = lax.all_gather(near, ('y', 'x'), axis=0, tiled=True)  84.3 us
    reduce_scatter x1, waiting for transfers between devices, shards(): lax.psum_scatter(full_terms, DIMS, scatter_dimension=1, tiled=True)  34 us
    all_to_all x1, blocking collectives, shards(): jax.lax.all_to_all(jnp.stack([queries for _ in range(jax.lax.psum(1, axis...  30.6 us
    gather x2, local copies, waits for them, and re-layouts, pair_products(): picked_queries = jnp.take(query_blocks, pair_ids // local_blocks, axis=0)  27.2 us
    dot_general x2, matrix products, pair_products(): jnp.einsum('gqc,gdc->gqd', picked_queries, picked_docs, preferred_element...  25.2 us
    gather x2, local copies, waits for them, and re-layouts, pair_products(): picked_docs = jnp.take(doc_side, pair_ids % local_blocks, axis=0)  17.4 us
  transfers between devices with their start and end apart: 3, of which 3 were waited for; matrix products, arithmetic and copies ran while one was open for 15% of the time, Pallas kernels for 0%

profile of v1, /device:TPU:2, one launch (start us, length us, event | category | flops | bytes accessed | tf_op | source)
XLA Modules:
  0.0 344.8 jit_solution(18074171448919336911)
XLA Ops:
  7.2 0.0 copy-start
  7.2 0.0 all-gather.2.cloned.1.call-start
  7.2 1.3 pad_maximum_fusion
  8.5 30.6 %all_to_all.5 = bf16[2,512,384]{2,1,0:T(8,128)(2,1)} all-to-all(bf16[2,512,384]{2,1,0:T(8,128)(2,1)S(1)} %pad_maximum_fusion), channel_id=1, replica_groups=mesh['y'=4,'x'=4,'zh'=2,'zl'=4,'c'=2] {'zh'}, dimensions={0} | all-to-all | bytes 1572864 | tf_op jit(solution)/shard_map/all_to_all | solution.py:18
  39.1 0.0 all-gather.2.cloned.1.call-update
  39.1 0.0 reduce-scatter.5.cloned.1.call-start
  39.2 0.7 fusion.12
  39.9 0.0 copy-done
  39.9 0.0 copy-start.2
  39.9 7.9 %gather_fusion.3 = bf16[96,128,384]{2,1,0:T(8,128)(2,1)} fusion(bf16[16,128,384]{2,1,0:T(8,128)(2,1)S(1)} %bitcast.67, s32[1024]{0:T(1024)S(1)} %get-tuple-element.10), kind=kCustom, calls=%fused_computation.3 | custom fusion | bytes 18874752 | tf_op jit(solution)/shard_map/jit(_take)/gather | solution.py:37
  47.8 0.0 copy-done.2
  47.8 84.3 %all-gather.2.cloned.1.call-done = bf16[16384,384]{1,0:T(8,128)(2,1)} async-done(((bf16[1024,384]{1,0:T(8,128)(2,1)}), bf16[16384,384]{1,0:T(8,128)(2,1)}) %all-gather.2.cloned.1.call-update) | async-done | bytes 12582928 | tf_op jit(solution)/shard_map/all_gather | solution.py:25
  132.1 12.5 %gather_fusion.2 = bf16[96,128,384]{2,1,0:T(8,128)(2,1)} fusion(bf16[128,128,384]{2,1,0:T(8,128)(2,1)} %bitcast.69, s32[1024]{0:T(1024)S(1)} %get-tuple-element.11), kind=kCustom, calls=%fused_computation.2 | custom fusion | bytes 18874752 | tf_op jit(solution)/shard_map/jit(_take)/gather | solution.py:36
  144.6 0.0 copy-start.1
  144.6 10.3 %fusion.5 = f32[96,128,128]{2,1,0:T(8,128)} fusion(bf16[96,128,384]{2,1,0:T(8,128)(2,1)} %gather_fusion.3, bf16[96,128,384]{2,1,0:T(8,128)(2,1)} %gather_fusion.2, pred[96]{0:T(512)(128)(4,1)S(1)} %get-tuple-element.7, pred[96]{0:T(512)(128)(4,1)S(1)} %get-tuple-element.6), kind=kOutput, calls=%fused_computation.9 | convolution fusion | flops 1217396736 | bytes 25166016 | tf_op jit(solution)/shard_map/gqc,gdc->gqd/dot_general | solution.py:38
  154.9 0.0 reduce-scatter.5.cloned.1.call-update
  155.0 0.2 reduce-scatter.3.cloned.1.call-start
  155.2 0.0 copy-done.1
  155.3 0.2 broadcast_select_fusion
  155.4 9.5 %gather_fusion.1 = bf16[144,128,384]{2,1,0:T(8,128)(2,1)} fusion(bf16[16,128,384]{2,1,0:T(8,128)(2,1)S(1)} %broadcast_select_fusion, s32[1024]{0:T(1024)S(1)} %pad_clamp_fusion.2), kind=kCustom, calls=%fused_computation.1 | custom fusion | bytes 28312128 | tf_op jit(solution)/shard_map/jit(_take)/gather | solution.py:37
  165.0 14.7 %gather_fusion = bf16[144,128,384]{2,1,0:T(8,128)(2,1)} fusion(bf16[128,128,384]{2,1,0:T(8,128)(2,1)} %bitcast.70, s32[1024]{0:T(1024)S(1)} %pad_clamp_fusion.3), kind=kCustom, calls=%fused_computation | custom fusion | bytes 28312128 | tf_op jit(solution)/shard_map/jit(_take)/gather | solution.py:36
  179.7 14.8 %fusion = f32[144,128,128]{2,1,0:T(8,128)} fusion(bf16[144,128,384]{2,1,0:T(8,128)(2,1)} %gather_fusion.1, bf16[144,128,384]{2,1,0:T(8,128)(2,1)} %gather_fusion, pred[144]{0:T(512)(128)(4,1)S(1)} %get-tuple-element.5, pred[144]{0:T(512)(128)(4,1)S(1)} %get-tuple-element.4), kind=kOutput, calls=%fused_computation.4 | convolution fusion | flops 1826095104 | bytes 37749024 | tf_op jit(solution)/shard_map/gqc,gdc->gqd/dot_general | solution.py:38
  194.5 0.0 reduce-scatter.3.cloned.1.call-update
  195.9 34.0 %reduce-scatter.5.cloned.1.call-done = f32[96,16,128]{2,1,0:T(8,128)} async-done(((f32[96,128,128]{2,1,0:T(8,128)}), f32[96,16,128]{2,1,0:T(8,128)}) %reduce-scatter.5.cloned.1.call-update) | async-done | bytes 786448 | tf_op jit(solution)/shard_map/reduce_scatter | solution.py:46
  229.9 2.2 select_bitcast_fusion.1
  232.1 103.7 %reduce-scatter.3.cloned.1.call-done = f32[144,16,128]{2,1,0:T(8,128)} async-done(((f32[144,128,128]{2,1,0:T(8,128)}), f32[144,16,128]{2,1,0:T(8,128)}) %reduce-scatter.3.cloned.1.call-update) | async-done | bytes 1179664 | tf_op jit(solution)/shard_map/reduce_scatter | solution.py:45
  335.8 2.5 select_bitcast_fusion
  (10 shorter events, 0.1 us)
Async XLA Ops:
  7.2 32.7 %copy-start = (bf16[2048,384]{1,0:T(8,128)(2,1)S(1)}, bf16[2048,384]{1,0:T(8,128)(2,1)}, u32[]{:S(2)}) copy-start(bf16[2048,384]{1,0:T(8,128)(2,1)} %param.7) | copy-start | bytes 4718596
  7.2 124.9 %all-gather.2.cloned.1.call-start = ((), (), s32[]{:S(2)}) async-start(), calls=%async_computation.3 | async-start | bytes 13369344 | tf_op jit(solution)/shard_map/all_gather | solution.py:25
  39.1 190.7 %reduce-scatter.5.cloned.1.call-start = ((), (), s32[]{:S(2)}) async-start(), calls=%async_computation.5 | async-start | bytes 7077888 | tf_op jit(solution)/shard_map/reduce_scatter | solution.py:46
  39.9 7.9 %copy-start.2 = (s32[1,96]{1,0:T(1,128)S(1)}, s32[1,96]{1,0:T(1,128)}, u32[]{:S(2)}) copy-start(s32[1,96]{1,0:T(1,128)} %param.10) | copy-start | bytes 1156
  144.6 10.6 %copy-start.1 = (s32[1,144]{1,0:T(1,128)S(1)}, s32[1,144]{1,0:T(1,128)}, u32[]{:S(2)}) copy-start(s32[1,144]{1,0:T(1,128)} %param.8) | copy-start | bytes 1732
  155.0 180.8 %reduce-scatter.3.cloned.1.call-start = ((), (), s32[]{:S(2)}) async-start(), calls=%async_computation.4 | async-start | bytes 10616832 | tf_op jit(solution)/shard_map/reduce_scatter | solution.py:45
Sparse Core Ops, SparseCore 0:
  39.3 92.7 all-gather.1
  155.1 74.7 reduce-scatter.4
  232.4 103.2 reduce-scatter.2
